TPU v7x, 32 devices: a whole 2x2x4 slice. The times are simulated.
32 devices in a mesh: groups: 2 (over y), cols: 4 (over z), slab: 2 (over x), rep: 2 (over core).
Axes of the slice: x: 2, y: 2, z: 4, core: 2. Of those that a mesh axis runs over, the one named last changes fastest.
Arguments:
- fields: bfloat16 [16, 8, 2048, 512], P('cols', 'groups', 'rep', 'slab'), parts along dimension 1, may hold values from -250 to 250
- stresses: bfloat16 [6, 8, 512, 128], P(None, 'groups', 'rep', 'slab'), parts along dimension 1, may hold values from -750 to 750
- planes: int32 [8], P('groups'), parts along dimension 0, may hold values from 0 to 2047, as said below
- active_masks: int32 [3, 6, 256], replicated, may hold values 0 or 1
Outputs:
- coefficients: float32 [3, 12, 256], P(None, 'groups', 'cols'), parts along dimension 1
- misfit: bfloat16 [6, 8, 512, 128], P(None, 'groups', 'rep', 'slab'), parts along dimension 1
There are 2 independent parts, one for each index of `groups`. A program takes and returns all parts, laid end to end along the dimension named above; an argument that names none is the same for every part. Nothing has to cross between parts.
Inputs may be any that keep to these rules, and one draw needn't show every extreme that they name: `planes`: sorted and distinct; either the first is 0 or the last is 2047.
All inputs are finite; a program needn't handle non-finite values.
Results may differ from a plain program's by a relative error of at most 0.0069.
Values may be sent and summed in bfloat16 or wider, within the bound.
No kernel may reach another device: no remote copies, remote signals or barrier semaphores. Data moves between devices by JAX's collectives and lax.ppermute only.
A program may use at most 128 MiB of HBM per device.

v0:
```python
import math
import jax
import jax.numpy as jnp
import numpy as np
from jax import lax
from jax.sharding import PartitionSpec as P

STRESS = 6
TERMS = 256
NY = 2048
PASSES = 3
ITERS = 3
ridge_weight = 0.05
epsilon = 1e-06


def extended(array, sides, width):
    for axis, dim in sides:
        count, length = (lax.axis_size(axis), array.shape[dim])
        up = [(i, (i + 1) % count) for i in range(count)]
        down = [(j, i) for i, j in up]
        last = lax.slice_in_dim(array, length - width, length, axis=dim)
        leading = lax.slice_in_dim(array, 0, width, axis=dim)
        before = lax.ppermute(last, axis, up)
        after = lax.ppermute(leading, axis, down)
        array = jnp.concatenate([before, array, after], axis=dim)
    return array


def kernel(spread):
    offsets = np.arange(13) - 6.0
    values = np.exp(-offsets * offsets / (2.0 * spread * spread))
    return values / values.sum()


def filter_table(cells, first_taps, second_taps):
    out_count = cells // 4
    table = np.zeros((cells + 10, 2, out_count), np.float32)
    for which, taps in ((0, first_taps), (1, second_taps)):
        for out_index in range(out_count):
            for tap_index in range(13):
                table[1 + tap_index + 4 * out_index, which, out_index] = taps[tap_index]
    return table


def library(narrow_part, broad_part):
    product = (
        narrow_part.astype(jnp.float32)[:, None, :] * broad_part.astype(jnp.float32)[None, :, :]
    )
    return product.astype(jnp.bfloat16).reshape(
        narrow_part.shape[0] * broad_part.shape[0], narrow_part.shape[1]
    )


def local(fields, stresses, planes, active_masks):
    chan_dev, plane_count, cells_x, cells_z = fields.shape
    coarse_x = cells_x // 4
    coarse_z = cells_z // 4
    row_count = plane_count * coarse_x * coarse_z
    col_devices = lax.axis_size("cols")
    column_index = lax.axis_index("cols")
    term_dev = TERMS // col_devices
    offset = column_index * term_dev
    samples = float(row_count * lax.axis_size("slab") * lax.axis_size("rep"))
    height = 2.0 * (planes.astype(jnp.float32) + 0.5) / NY - 1.0
    root_weight = jnp.sqrt(1.2 - height * height)
    padded = extended(fields, (("slab", 3), ("rep", 2)), 5)
    widened = padded.astype(jnp.float32)
    narrow_taps = kernel(1.5)
    broad_taps = kernel(3.0)
    span_table = jnp.asarray(filter_table(cells_z, narrow_taps, broad_taps))
    stream_table = jnp.asarray(
        np.transpose(filter_table(cells_x, narrow_taps, broad_taps), (1, 0, 2))
    )
    along_span = jnp.einsum("cpxz,zsn->cpxsn", widened, span_table, precision=lax.Precision.HIGHEST)
    filtered = jnp.einsum(
        "cpxsn,sxm->scpmn", along_span, stream_table, precision=lax.Precision.HIGHEST
    )
    narrow = filtered[0]
    broader = filtered[1]
    narrow_set = narrow.astype(jnp.bfloat16).reshape(chan_dev, row_count)
    broad_set = (
        (broader * root_weight[None, :, None, None])
        .astype(jnp.bfloat16)
        .reshape(chan_dev, row_count)
    )
    weighted = (stresses.astype(jnp.float32) * root_weight[None, :, None, None]).astype(
        jnp.bfloat16
    )
    weighted = weighted.reshape(STRESS, row_count)
    block_rows = math.gcd(row_count, 4096)
    block_count = row_count // block_rows
    narrow_all, broad_all = (
        lax.all_gather(narrow_set, "cols", axis=0, tiled=True),
        lax.all_gather(broad_set, "cols", axis=0, tiled=True),
    )

    def gram_step(block_index, carry):
        gram_acc, rhs_acc = carry
        start = block_index * block_rows
        narrow_piece = lax.dynamic_slice_in_dim(narrow_all, start, block_rows, 1)
        broad_piece = lax.dynamic_slice_in_dim(broad_all, start, block_rows, 1)
        own_piece = lax.dynamic_slice_in_dim(narrow_set, start, block_rows, 1)
        all_terms = library(narrow_piece, broad_piece)
        own_terms = library(own_piece, broad_piece)
        weighted_piece = lax.dynamic_slice_in_dim(weighted, start, block_rows, 1)
        gram_acc = gram_acc + jnp.einsum(
            "ir,jr->ij", own_terms, all_terms, preferred_element_type=jnp.float32
        )
        rhs_acc = rhs_acc + jnp.einsum(
            "ir,kr->ik", own_terms, weighted_piece, preferred_element_type=jnp.float32
        )
        return (gram_acc, rhs_acc)

    gram_block, rhs_block = lax.fori_loop(
        0,
        block_count,
        gram_step,
        (jnp.zeros((term_dev, TERMS), jnp.float32), jnp.zeros((term_dev, STRESS), jnp.float32)),
    )
    gram_block, rhs_block = lax.psum((gram_block, rhs_block), ("slab", "rep"))
    diag_own = jnp.diagonal(lax.dynamic_slice_in_dim(gram_block, offset, term_dev, 1))
    diag_all, rhs_all = (
        lax.all_gather(diag_own, "cols", axis=0, tiled=True),
        lax.all_gather(rhs_block, "cols", axis=0, tiled=True),
    )
    column_scale = 1.0 / jnp.sqrt(diag_all / samples + epsilon)
    scale_own = lax.dynamic_slice_in_dim(column_scale, offset, term_dev, 0)
    normal_rows = scale_own[:, None] * gram_block * column_scale[None, :] / samples
    target_norm = column_scale[None, :] * rhs_all.T / samples
    results = []

    def apply_pieces(vector_own, active_own):
        gathered = lax.all_gather(active_own * vector_own, "cols", axis=1, tiled=True)
        product = jnp.einsum("kl,il->ki", gathered, normal_rows, precision=lax.Precision.HIGHEST)
        return active_own * product + ridge_weight * vector_own

    def norm_of(vector_own):
        return lax.psum(jnp.sum(vector_own * vector_own, axis=1), "cols")

    target_own = lax.dynamic_slice_in_dim(target_norm, offset, term_dev, 1)
    solution_own = jnp.zeros((STRESS, term_dev), jnp.float32)
    for pass_index in range(PASSES):
        active_own = lax.dynamic_slice_in_dim(
            active_masks[pass_index].astype(jnp.float32), offset, term_dev, 1
        )
        solution_own = active_own * solution_own
        remain = active_own * target_own - apply_pieces(solution_own, active_own)
        direction = remain
        norm_now = norm_of(remain)
        for turn_index in range(ITERS):
            applied = apply_pieces(direction, active_own)
            curve_sum = lax.psum(jnp.sum(direction * applied, axis=1), "cols")
            step_size = norm_now / (curve_sum + epsilon)
            solution_own = solution_own + step_size[:, None] * direction
            remain = remain - step_size[:, None] * applied
            norm_next = norm_of(remain)
            direction = remain + (norm_next / (norm_now + epsilon))[:, None] * direction
            norm_now = norm_next
        results.append(solution_own)
    final_solution = lax.all_gather(solution_own, "cols", axis=1, tiled=True)
    coefficients = jnp.stack(results)
    final_weights = (column_scale[None, :] * final_solution).astype(jnp.bfloat16)

    def misfit_step(block_index, misfit_acc):
        start = block_index * block_rows
        narrow_piece = lax.dynamic_slice_in_dim(narrow_all, start, block_rows, 1)
        broad_piece = lax.dynamic_slice_in_dim(broad_all, start, block_rows, 1)
        all_terms = library(narrow_piece, broad_piece)
        predicted = jnp.dot(final_weights, all_terms, preferred_element_type=jnp.float32)
        weighted_piece = lax.dynamic_slice_in_dim(weighted, start, block_rows, 1)
        piece_misfit = (weighted_piece.astype(jnp.float32) - predicted).astype(jnp.bfloat16)
        return lax.dynamic_update_slice_in_dim(misfit_acc, piece_misfit, start, 1)

    misfit = lax.fori_loop(
        0, block_count, misfit_step, jnp.zeros((STRESS, row_count), jnp.bfloat16)
    )
    misfit = misfit.reshape(STRESS, plane_count, coarse_x, coarse_z)
    return (coefficients, misfit)


def solution(mesh):
    placed = (
        P("cols", "groups", "rep", "slab"),
        P(None, "groups", "rep", "slab"),
        P("groups"),
        P(),
    )
    return jax.shard_map(
        local,
        mesh=mesh,
        in_specs=placed,
        out_specs=(P(None, "groups", "cols"), P(None, "groups", "rep", "slab")),
        check_vma=False,
    )
```

profile of v0, /device:TPU:0, one launch (start us, length us, event | category | flops | bytes accessed | tf_op | source)
XLA Modules:
  0.0 648.6 jit_solution(8364757962872632828)
XLA Ops:
  7.2 11.5 %copy.51 = bf16[4,4,1024,256]{2,3,1,0:T(8,128)(2,1)} copy(bf16[4,4,1024,256]{3,2,1,0:T(8,128)(2,1)} %param.10) | data formatting | bytes 16777216 | tf_op args[0]
  19.8 3.0 collective-permute-start
  22.9 7.1 %collective-permute-done = bf16[4,4,1024,5]{2,3,1,0:T(8,128)(2,1)S(1)} collective-permute-done((bf16[4,4,1024,5]{2,3,1,0:T(8,128)(2,1)S(1)}, bf16[4,4,1024,5]{2,3,1,0:T(8,128)(2,1)S(1)}, u32[]{:S(2)}, u32[]{:S(2)}) %collective-permute-start) | collective-permute-done | bytes 163872 | tf_op jit(solution)/shard_map/ppermute | solution.py:24
  30.0 4.8 collective-permute-done.1
  34.7 5.5 pad_maximum_fusion
  40.3 3.5 copy-done
  47.7 18.5 %concatenate.11 = bf16[4,4,1034,266]{2,3,1,0:T(8,128)(2,1)} concatenate(bf16[4,4,5,266]{2,3,1,0:T(8,128)(2,1)S(1)} %copy.56, bf16[4,4,1024,266]{2,3,1,0:T(8,128)(2,1)} %copy-done, bf16[4,4,5,266]{2,3,1,0:T(8,128)(2,1)S(1)} %copy.57), dimensions={2} | concatenate | bytes 17602816 | tf_op jit(solution)/shard_map/concatenate | solution.py:26
  66.2 10.5 %fusion.5 = f32[4,4,1034,2,64]{2,4,1,0,3:T(8,128)S(1)} fusion(f32[266,2,64,1,1]{0,2,4,3,1:T(8,128)S(1)} %copy-done.5, bf16[4,4,1034,266]{2,3,1,0:T(8,128)(2,1)} %concatenate.11), kind=kOutput, calls=%fused_computation.17 | convolution fusion | flops 6759481344 | bytes 17408128 | tf_op jit(solution)/shard_map/cpxz,zsn->cpxsn/dot_general | solution.py:75
  76.7 8.7 %convolution_bitcast_fusion.1 = f32[2,4,4,256,64]{3,4,2,1,0:T(8,128)S(1)} fusion(f32[4,4,1034,2,64]{2,4,1,0,3:T(8,128)S(1)} %fusion.5, f32[2,1034,256,1,1]{2,1,4,3,0:T(8,128)S(1)} %copy-done.3), kind=kOutput, calls=%fused_computation.20 | convolution fusion | flops 6505365504 | bytes 12685312 | tf_op jit(solution)/shard_map/cpxsn,sxm->scpmn/dot_general | solution.py:76
  85.4 1.3 copy-done.1
  89.5 1.3 slice.46
  91.3 1.5 reshape.109
  94.4 2.3 reshape.96
  97.4 39.6 %all-gather.19.cloned.1.call-done = bf16[4,4,65536]{2,1,0:T(4,128)(2,1)} async-done(((bf16[1,4,65536]{2,1,0:T(4,128)(2,1)}), bf16[4,4,65536]{2,1,0:T(4,128)(2,1)}) %all-gather.19.cloned.1.call-update) | async-done | bytes 2097168 | tf_op jit(solution)/shard_map/all_gather | solution.py:95
  137.1 2.8 reshape.108
  139.9 43.4 %all-gather.21.cloned.1.call-done = bf16[4,4,65536]{2,1,0:T(4,128)(2,1)} async-done(((bf16[1,4,65536]{2,1,0:T(4,128)(2,1)}), bf16[4,4,65536]{2,1,0:T(4,128)(2,1)}) %all-gather.21.cloned.1.call-update) | async-done | bytes 2097168 | tf_op jit(solution)/shard_map/all_gather | solution.py:94
  183.3 2.8 reshape.110
  186.1 53.2 %while.30 = (s32[]{:T(128)}, f32[64,256]{1,0:T(8,128)S(1)}, f32[64,6]{0,1:T(8,128)S(1)}, bf16[4,65536]{1,0:T(4,128)(2,1)S(1)}, bf16[16,65536]{1,0:T(8,128)(2,1)}...) while((s32[]{:T(128)}, f32[64,256]{1,0:T(8,128)S(1)}, ...), condition=%wide.region_1.0_spmd.clone, body=%wide.region_0.0_spmd.clone.sunk | while | flops 140165888 | bytes 7703730 | solution.py:115
  240.0 13.1 %all-gather.3 = f32[4,64,6]{1,2,0:T(8,128)S(1)} all-gather(f32[1,64,6]{1,2,0:T(8,128)S(1)} %fusion.29), channel_id=1, replica_groups=mesh['groups'=2,'cols'=4,'slab'=2,'rep'=2] {'cols'}, dimensions={0}, use_global_device_ids=true | all-gather | bytes 7680 | tf_op jit(solution)/shard_map/all_gather | solution.py:134
  254.5 5.7 psum.141
  260.1 13.1 %all-gather.2 = f32[4,64,6]{1,2,0:T(8,128)S(1)} all-gather(f32[1,64,6]{1,2,0:T(8,128)S(1)} %bitcast.248), channel_id=1, replica_groups=mesh['groups'=2,'cols'=4,'slab'=2,'rep'=2] {'cols'}, dimensions={0}, use_global_device_ids=true | all-gather | bytes 7680 | tf_op jit(solution)/shard_map/all_gather | solution.py:125
  275.3 9.5 %all-reduce = f32[256]{0:T(256)S(1)} all-reduce(f32[256]{0:T(256)S(1)} %dynamic-update-slice), channel_id=1, replica_groups=mesh['groups'=2,'cols'=4,'slab'=2,'rep'=2] {'cols'}, use_global_device_ids=true, to_apply=%add | all-reduce | flops 256 | bytes 2048
  286.0 13.1 %all-gather.4 = f32[4,64,6]{1,2,0:T(8,128)S(1)} all-gather(f32[1,64,6]{1,2,0:T(8,128)S(1)} %multiply_bitcast_fusion.10), channel_id=1, replica_groups=mesh['groups'=2,'cols'=4,'slab'=2,'rep'=2] {'cols'}, dimensions={0}, use_global_device_ids=true | all-gather | bytes 7680 | tf_op jit(solution)/shard_map/all_gather | solution.py:134
  300.5 9.3 %all-reduce.3 = (f32[6]{0:T(128)S(1)}, f32[6]{0:T(128)S(1)}) all-reduce(f32[6]{0:T(128)S(1)} %get-tuple-element.274, f32[6]{0:T(128)S(1)} %get-tuple-element.273), channel_id=1, replica_groups=mesh['groups'=2,'cols'=4,'slab'=2,'rep'=2] {'cols'}, use_global_device_ids=true, to_apply=%region_5.6 | all-reduce | flops 12 | bytes 96 | tf_op jit(solution)/shard_map/psum | solution.py:139
  309.9 9.5 %psum.144 = f32[6]{0:T(128)S(1)} all-reduce(f32[6]{0:T(128)S(1)} %get-tuple-element.327), channel_id=1, replica_groups=mesh['groups'=2,'cols'=4,'slab'=2,'rep'=2] {'cols'}, use_global_device_ids=true, to_apply=%region_9.10 | all-reduce | flops 6 | bytes 48 | tf_op jit(solution)/shard_map/psum | solution.py:139
  319.5 13.1 %all-gather.5 = f32[4,64,6]{1,2,0:T(8,128)S(1)} all-gather(f32[1,64,6]{1,2,0:T(8,128)S(1)} %get-tuple-element.325), channel_id=1, replica_groups=mesh['groups'=2,'cols'=4,'slab'=2,'rep'=2] {'cols'}, dimensions={0}, use_global_device_ids=true | all-gather | bytes 7680 | tf_op jit(solution)/shard_map/all_gather | solution.py:134
  333.9 9.2 %psum.145 = f32[6]{0:T(128)S(1)} all-reduce(f32[6]{0:T(128)S(1)} %get-tuple-element.341), channel_id=1, replica_groups=mesh['groups'=2,'cols'=4,'slab'=2,'rep'=2] {'cols'}, use_global_device_ids=true, to_apply=%region_11.12 | all-reduce | flops 6 | bytes 48 | tf_op jit(solution)/shard_map/psum | solution.py:153
  343.4 9.5 %psum.146 = f32[6]{0:T(128)S(1)} all-reduce(f32[6]{0:T(128)S(1)} %multiply_reduce_fusion.10), channel_id=1, replica_groups=mesh['groups'=2,'cols'=4,'slab'=2,'rep'=2] {'cols'}, use_global_device_ids=true, to_apply=%region_13.14 | all-reduce | flops 6 | bytes 48 | tf_op jit(solution)/shard_map/psum | solution.py:139
  352.9 13.1 %all-gather.6 = f32[4,64,6]{1,2,0:T(8,128)S(1)} all-gather(f32[1,64,6]{1,2,0:T(8,128)S(1)} %get-tuple-element.323), channel_id=1, replica_groups=mesh['groups'=2,'cols'=4,'slab'=2,'rep'=2] {'cols'}, dimensions={0}, use_global_device_ids=true | all-gather | bytes 7680 | tf_op jit(solution)/shard_map/all_gather | solution.py:134
  367.3 9.2 %psum.147 = f32[6]{0:T(128)S(1)} all-reduce(f32[6]{0:T(128)S(1)} %fusion.25), channel_id=1, replica_groups=mesh['groups'=2,'cols'=4,'slab'=2,'rep'=2] {'cols'}, use_global_device_ids=true, to_apply=%region_15.16 | all-reduce | flops 6 | bytes 48 | tf_op jit(solution)/shard_map/psum | solution.py:153
  376.7 13.1 %all-gather.7 = f32[4,64,6]{1,2,0:T(8,128)S(1)} all-gather(f32[1,64,6]{1,2,0:T(8,128)S(1)} %get-tuple-element.321), channel_id=1, replica_groups=mesh['groups'=2,'cols'=4,'slab'=2,'rep'=2] {'cols'}, dimensions={0}, use_global_device_ids=true | all-gather | bytes 7680 | tf_op jit(solution)/shard_map/all_gather | solution.py:134
  391.1 13.1 %all-gather.8 = f32[4,64,6]{1,2,0:T(8,128)S(1)} all-gather(f32[1,64,6]{1,2,0:T(8,128)S(1)} %multiply_bitcast_fusion.6), channel_id=1, replica_groups=mesh['groups'=2,'cols'=4,'slab'=2,'rep'=2] {'cols'}, dimensions={0}, use_global_device_ids=true | all-gather | bytes 7680 | tf_op jit(solution)/shard_map/all_gather | solution.py:134
  405.5 9.5 %all-reduce.2 = (f32[6]{0:T(128)S(1)}, f32[6]{0:T(128)S(1)}) all-reduce(f32[6]{0:T(128)S(1)} %get-tuple-element.272, f32[6]{0:T(128)S(1)} %get-tuple-element.271), channel_id=1, replica_groups=mesh['groups'=2,'cols'=4,'slab'=2,'rep'=2] {'cols'}, use_global_device_ids=true, to_apply=%region_17.18 | all-reduce | flops 12 | bytes 96 | tf_op jit(solution)/shard_map/psum | solution.py:139
  415.2 9.2 %psum.150 = f32[6]{0:T(128)S(1)} all-reduce(f32[6]{0:T(128)S(1)} %get-tuple-element.319), channel_id=1, replica_groups=mesh['groups'=2,'cols'=4,'slab'=2,'rep'=2] {'cols'}, use_global_device_ids=true, to_apply=%region_21.22 | all-reduce | flops 6 | bytes 48 | tf_op jit(solution)/shard_map/psum | solution.py:139
  424.5 13.1 %all-gather.9 = f32[4,64,6]{1,2,0:T(8,128)S(1)} all-gather(f32[1,64,6]{1,2,0:T(8,128)S(1)} %get-tuple-element.317), channel_id=1, replica_groups=mesh['groups'=2,'cols'=4,'slab'=2,'rep'=2] {'cols'}, dimensions={0}, use_global_device_ids=true | all-gather | bytes 7680 | tf_op jit(solution)/shard_map/all_gather | solution.py:134
  438.9 9.5 %psum.151 = f32[6]{0:T(128)S(1)} all-reduce(f32[6]{0:T(128)S(1)} %get-tuple-element.344), channel_id=1, replica_groups=mesh['groups'=2,'cols'=4,'slab'=2,'rep'=2] {'cols'}, use_global_device_ids=true, to_apply=%region_23.24 | all-reduce | flops 6 | bytes 48 | tf_op jit(solution)/shard_map/psum | solution.py:153
  448.7 9.2 %psum.152 = f32[6]{0:T(128)S(1)} all-reduce(f32[6]{0:T(128)S(1)} %multiply_reduce_fusion.5), channel_id=1, replica_groups=mesh['groups'=2,'cols'=4,'slab'=2,'rep'=2] {'cols'}, use_global_device_ids=true, to_apply=%region_25.26 | all-reduce | flops 6 | bytes 48 | tf_op jit(solution)/shard_map/psum | solution.py:139
  458.0 13.1 %all-gather.10 = f32[4,64,6]{1,2,0:T(8,128)S(1)} all-gather(f32[1,64,6]{1,2,0:T(8,128)S(1)} %get-tuple-element.315), channel_id=1, replica_groups=mesh['groups'=2,'cols'=4,'slab'=2,'rep'=2] {'cols'}, dimensions={0}, use_global_device_ids=true | all-gather | bytes 7680 | tf_op jit(solution)/shard_map/all_gather | solution.py:134
  472.4 9.5 %psum.153 = f32[6]{0:T(128)S(1)} all-reduce(f32[6]{0:T(128)S(1)} %fusion.26), channel_id=1, replica_groups=mesh['groups'=2,'cols'=4,'slab'=2,'rep'=2] {'cols'}, use_global_device_ids=true, to_apply=%region_27.28 | all-reduce | flops 6 | bytes 48 | tf_op jit(solution)/shard_map/psum | solution.py:153
  482.0 13.1 %all-gather.11 = f32[4,64,6]{1,2,0:T(8,128)S(1)} all-gather(f32[1,64,6]{1,2,0:T(8,128)S(1)} %get-tuple-element.313), channel_id=1, replica_groups=mesh['groups'=2,'cols'=4,'slab'=2,'rep'=2] {'cols'}, dimensions={0}, use_global_device_ids=true | all-gather | bytes 7680 | tf_op jit(solution)/shard_map/all_gather | solution.py:134
  495.5 13.1 %all-gather.12 = f32[4,64,6]{1,2,0:T(8,128)S(1)} all-gather(f32[1,64,6]{1,2,0:T(8,128)S(1)} %multiply_bitcast_fusion.2), channel_id=1, replica_groups=mesh['groups'=2,'cols'=4,'slab'=2,'rep'=2] {'cols'}, dimensions={0}, use_global_device_ids=true | all-gather | bytes 7680 | tf_op jit(solution)/shard_map/all_gather | solution.py:134
  509.1 9.2 %all-reduce.1 = (f32[6]{0:T(128)S(1)}, f32[6]{0:T(128)S(1)}) all-reduce(f32[6]{0:T(128)S(1)} %get-tuple-element.270, f32[6]{0:T(128)S(1)} %get-tuple-element.269), channel_id=1, replica_groups=mesh['groups'=2,'cols'=4,'slab'=2,'rep'=2] {'cols'}, use_global_device_ids=true, to_apply=%region_29.30 | all-reduce | flops 12 | bytes 96 | tf_op jit(solution)/shard_map/psum | solution.py:139
  518.5 9.5 %psum.156 = f32[6]{0:T(128)S(1)} all-reduce(f32[6]{0:T(128)S(1)} %get-tuple-element.311), channel_id=1, replica_groups=mesh['groups'=2,'cols'=4,'slab'=2,'rep'=2] {'cols'}, use_global_device_ids=true, to_apply=%region_33.34 | all-reduce | flops 6 | bytes 48 | tf_op jit(solution)/shard_map/psum | solution.py:139
  528.1 13.1 %all-gather.13 = f32[4,64,6]{1,2,0:T(8,128)S(1)} all-gather(f32[1,64,6]{1,2,0:T(8,128)S(1)} %get-tuple-element.309), channel_id=1, replica_groups=mesh['groups'=2,'cols'=4,'slab'=2,'rep'=2] {'cols'}, dimensions={0}, use_global_device_ids=true | all-gather | bytes 7680 | tf_op jit(solution)/shard_map/all_gather | solution.py:134
  541.7 9.2 %psum.157 = f32[6]{0:T(128)S(1)} all-reduce(f32[6]{0:T(128)S(1)} %get-tuple-element.347), channel_id=1, replica_groups=mesh['groups'=2,'cols'=4,'slab'=2,'rep'=2] {'cols'}, use_global_device_ids=true, to_apply=%region_35.36 | all-reduce | flops 6 | bytes 48 | tf_op jit(solution)/shard_map/psum | solution.py:153
  551.1 9.5 %psum.158 = f32[6]{0:T(128)S(1)} all-reduce(f32[6]{0:T(128)S(1)} %multiply_reduce_fusion), channel_id=1, replica_groups=mesh['groups'=2,'cols'=4,'slab'=2,'rep'=2] {'cols'}, use_global_device_ids=true, to_apply=%region_37.38 | all-reduce | flops 6 | bytes 48 | tf_op jit(solution)/shard_map/psum | solution.py:139
  560.7 13.1 %all-gather.14 = f32[4,64,6]{1,2,0:T(8,128)S(1)} all-gather(f32[1,64,6]{1,2,0:T(8,128)S(1)} %get-tuple-element.307), channel_id=1, replica_groups=mesh['groups'=2,'cols'=4,'slab'=2,'rep'=2] {'cols'}, dimensions={0}, use_global_device_ids=true | all-gather | bytes 7680 | tf_op jit(solution)/shard_map/all_gather | solution.py:134
  574.3 9.2 %psum.159 = f32[6]{0:T(128)S(1)} all-reduce(f32[6]{0:T(128)S(1)} %fusion.27), channel_id=1, replica_groups=mesh['groups'=2,'cols'=4,'slab'=2,'rep'=2] {'cols'}, use_global_device_ids=true, to_apply=%region_39.40 | all-reduce | flops 6 | bytes 48 | tf_op jit(solution)/shard_map/psum | solution.py:153
  583.6 13.4 %all-gather.15 = f32[4,64,6]{1,2,0:T(8,128)S(1)} all-gather(f32[1,64,6]{1,2,0:T(8,128)S(1)} %bitcast.246), channel_id=1, replica_groups=mesh['groups'=2,'cols'=4,'slab'=2,'rep'=2] {'cols'}, dimensions={0}, use_global_device_ids=true | all-gather | bytes 7680 | tf_op jit(solution)/shard_map/all_gather | solution.py:161
  597.2 41.2 %while.29 = (s32[]{:T(128)}, bf16[6,65536]{1,0:T(8,128)(2,1)S(1)}, bf16[6,65536]{1,0:T(8,128)(2,1)}, bf16[16,65536]{1,0:T(8,128)(2,1)}, bf16[16,65536]{1,0:T(8,1...) while((s32[]{:T(128)}, bf16[6,65536]{1,0:T(8,128)(2,1)S(1)}, ...), condition=%wide.region_41.42_spmd, body=%wide.region_40.41_spmd.sunk | while | flops 14884870 | bytes 5623963 | solution.py:175
  598.6 1.2 fusion.73
  601.1 1.2 fusion.73
  603.7 1.2 fusion.73
  606.3 1.2 fusion.73
  608.9 1.2 fusion.73
  611.4 1.2 fusion.73
  616.6 1.2 fusion.73
  619.1 1.2 fusion.73
  626.9 1.2 fusion.73
  629.4 1.2 fusion.73
  634.6 1.2 fusion.73
  637.1 1.2 fusion.73
  638.4 1.6 reshape.97
  640.0 1.4 copy.76
  (267 shorter events, 107.4 us)
Async XLA Ops:
  7.2 129.9 %all-gather.19.cloned.1.call-start = ((), (), s32[]{:S(2)}) async-start(), calls=%async_computation.1 | async-start | bytes 2621440 | tf_op jit(solution)/shard_map/all_gather | solution.py:95
  19.8 10.1 %collective-permute-start = (bf16[4,4,1024,5]{2,3,1,0:T(8,128)(2,1)S(1)}, bf16[4,4,1024,5]{2,3,1,0:T(8,128)(2,1)S(1)}, u32[]{:S(2)}, u32[]{:S(2)}) collective-permute-start(bf16[4,4,1024,5]{2,3,1,0:T(8,128)(2,1)S(1)} %get-tuple-element.335), channel_id=1, source_target_pairs={{0,2},{2,0},{1,3},{3,1},{4,6},{6,4},{5,7},{7,5},{8,10},{10,8},{9,1... | collective-permute-start | bytes 491528 | tf_op jit(solution)/shard_map/ppermute | solution.py:24
  22.8 11.9 %collective-permute-start.1 = (bf16[4,4,1024,5]{2,3,1,0:T(8,128)(2,1)S(1)}, bf16[4,4,1024,5]{2,3,1,0:T(8,128)(2,1)S(1)}, u32[]{:S(2)}, u32[]{:S(2)}) collective-permute-start(bf16[4,4,1024,5]{2,3,1,0:T(8,128)(2,1)S(1)} %get-tuple-element.336), channel_id=1, source_target_pairs={{2,0},{0,2},{3,1},{1,3},{6,4},{4,6},{7,5},{5,7},{10,8},{8,10},{11,... | collective-permute-start | bytes 491528 | tf_op jit(solution)/shard_map/ppermute | solution.py:25
  40.3 3.5 copy-start
  44.4 1.8 copy-start.8
  45.0 1.5 collective-permute-start.2
  45.6 1.5 collective-permute-start.3
  47.7 18.5 %copy-start.5 = (f32[266,2,64,1,1]{0,2,4,3,1:T(8,128)S(1)}, f32[266,2,64,1,1]{0,2,4,3,1:T(8,128)}, u32[]{:S(2)}) copy-start(f32[266,2,64,1,1]{0,2,4,3,1:T(8,128)} %constant.133) | copy-start | bytes 408580
  66.2 10.5 %copy-start.3 = (f32[2,1034,256,1,1]{2,1,4,3,0:T(8,128)S(1)}, f32[2,1034,256,1,1]{2,1,4,3,0:T(8,128)}, u32[]{:S(2)}) copy-start(f32[2,1034,256,1,1]{2,1,4,3,0:T(8,128)} %constant.134) | copy-start | bytes 6352900
  85.4 1.4 copy-start.1
  89.4 3.7 copy-start.4
  89.4 93.9 %all-gather.21.cloned.1.call-start = ((), (), s32[]{:S(2)}) async-start(), calls=%async_computation.2 | async-start | bytes 2621440 | tf_op jit(solution)/shard_map/all_gather | solution.py:94
  92.8 180.5 %all-reduce.6.cloned.1.call-start = ((), (), s32[]{:S(2)}) async-start(), calls=%async_computation | async-start | bytes 131072 | tf_op jit(solution)/shard_map/psum | solution.py:121
  93.5 3.2 copy-start.6
  186.1 67.1 %copy-start.9 = (u32[32]{0:T(128)S(1)}, u32[32]{0:T(128)}, u32[]{:S(2)}) copy-start(u32[32]{0:T(128)} %constant.129) | copy-start | bytes 388
  239.3 0.6 copy-start.2
  273.4 221.9 %copy-start.7 = (f32[64,256]{1,0:T(8,128)S(1)}, f32[64,256]{1,0:T(8,128)}, u32[]{:S(2)}) copy-start(f32[64,256]{1,0:T(8,128)} %all-reduce.6.cloned.1.call-done) | copy-start | bytes 196612
Sparse Core Ops, SparseCore 0:
  89.5 47.4 all-gather.18
  138.6 44.6 all-gather.20
  240.1 29.7 all-reduce.5
where the time goes:
time: 652 us; the launch traced here: 649 us
  blocking collectives  340 us (52%)
  waiting for transfers between devices  94.9 us (15%)
  matrix products  79.3 us (12%)
  local copies, waits for them, and re-layouts  61 us (9%)
  other arithmetic  54.1 us (8%)
  between operations  14.7 us (2%)
    all_gather x12, blocking collectives, apply_pieces(): lax.all_gather(active_own * vector_own, 'cols', axis=1, tiled=True)  158 us
    psum x9, blocking collectives, norm_of(): return lax.psum(jnp.sum(vector_own * vector_own, axis=1), 'cols')  84.5 us
    psum x6, blocking collectives, local(): curve_sum = lax.psum(jnp.sum(direction * applied, axis=1), 'cols')  56.1 us
    all_gather x1, waiting for transfers between devices, local(): lax.all_gather(narrow_set, 'cols', axis=0, tiled=True)  43.4 us
    all_gather x1, waiting for transfers between devices, local(): lax.all_gather(broad_set, 'cols', axis=0, tiled=True)  39.6 us
    unnamed x42, local copies, waits for them, and re-layouts  27.5 us
    dot_general x16, matrix products, misfit_step(): jnp.dot(final_weights, all_terms, preferred_element_type=jnp.float32)  19.7 us
    concatenate x1, local copies, waits for them, and re-layouts, extended(): array = jnp.concatenate([before, array, after], axis=dim)  18.5 us
  transfers between devices with their start and end apart: 7, of which 4 were waited for; matrix products, arithmetic and copies ran while one was open for 2% of the time, Pallas kernels for 0%

commit v1 on v0

--- a/solution.py
+++ b/solution.py
@@ -12,6 +12,19 @@
 ITERS = 3
 ridge_weight = 0.05
 epsilon = 1e-06
+
+
+def collect(array, axis, dim):
+    ways = lax.axis_size(axis)
+    up = [(d, (d + 1) % ways) for d in range(ways)]
+    down = [(d, (d - 1) % ways) for d in range(ways)]
+    earlier, later = ([array], [array])
+    for _ in range(ways // 2):
+        earlier.append(lax.ppermute(earlier[-1], axis, up))
+    for _ in range((ways - 1) // 2):
+        later.append(lax.ppermute(later[-1], axis, down))
+    line = jnp.concatenate([*earlier[::-1], *later[1:]], axis=dim)
+    return jnp.roll(line, (lax.axis_index(axis) - ways // 2) * array.shape[dim], axis=dim)
 
 
 def extended(array, sides, width):
@@ -122,7 +135,7 @@
     diag_own = jnp.diagonal(lax.dynamic_slice_in_dim(gram_block, offset, term_dev, 1))
     diag_all, rhs_all = (
         lax.all_gather(diag_own, "cols", axis=0, tiled=True),
-        lax.all_gather(rhs_block, "cols", axis=0, tiled=True),
+        collect(rhs_block, "cols", 0),
     )
     column_scale = 1.0 / jnp.sqrt(diag_all / samples + epsilon)
     scale_own = lax.dynamic_slice_in_dim(column_scale, offset, term_dev, 0)

time: 652 us -> 650 us (level)
  blocking collectives: 340 us -> 329 us
    all_gather x1 -> x0, blocking collectives: 13.1 us -> none  [local(): lax.all_gather(rhs_block, 'cols', axis=0, tiled=True)]
    unnamed x42 -> x41, local copies, waits for them, and re-layouts: 27.5 us -> 27.4 us
  transfers between devices with their start and end apart: 7 -> 10, of which waited for: 4 -> 6; matrix products, arithmetic and copies ran while one was open for 2% -> 2% of each run, Pallas kernels for 0% -> 0%
where the time goes in v1:
time: 650 us; the launch traced here: 646 us
  blocking collectives  329 us (51%)
  waiting for transfers between devices  99.6 us (15%)
  matrix products  79.3 us (12%)
  local copies, waits for them, and re-layouts  61 us (9%)
  other arithmetic  54.1 us (8%)
  between operations  14.8 us (2%)
  starting transfers between devices  7.9 us (1%)
    all_gather x12, blocking collectives, apply_pieces(): lax.all_gather(active_own * vector_own, 'cols', axis=1, tiled=True)  157 us
    psum x9, blocking collectives, norm_of(): return lax.psum(jnp.sum(vector_own * vector_own, axis=1), 'cols')  85.4 us
    psum x6, blocking collectives, local(): curve_sum = lax.psum(jnp.sum(direction * applied, axis=1), 'cols')  54.3 us
    all_gather x1, waiting for transfers between devices, local(): lax.all_gather(narrow_set, 'cols', axis=0, tiled=True)  43.4 us
    all_gather x1, waiting for transfers between devices, local(): lax.all_gather(broad_set, 'cols', axis=0, tiled=True)  39.6 us
    unnamed x41, local copies, waits for them, and re-layouts  27.4 us
    dot_general x16, matrix products, misfit_step(): jnp.dot(final_weights, all_terms, preferred_element_type=jnp.float32)  19.7 us
    concatenate x1, local copies, waits for them, and re-layouts, extended(): array = jnp.concatenate([before, array, after], axis=dim)  18.5 us
  transfers between devices with their start and end apart: 10, of which 6 were waited for; matrix products, arithmetic and copies ran while one was open for 2% of the time, Pallas kernels for 0%

profile of v1, /device:TPU:0, one launch (start us, length us, event | category | flops | bytes accessed | tf_op | source)
XLA Modules:
  0.0 646.4 jit_solution(5297748772696625126)
XLA Ops:
  7.2 11.5 %copy.48 = bf16[4,4,1024,256]{2,3,1,0:T(8,128)(2,1)} copy(bf16[4,4,1024,256]{3,2,1,0:T(8,128)(2,1)} %param.10) | data formatting | bytes 16777216 | tf_op args[0]
  19.8 3.0 collective-permute-start
  22.9 7.1 %collective-permute-done = bf16[4,4,1024,5]{2,3,1,0:T(8,128)(2,1)S(1)} collective-permute-done((bf16[4,4,1024,5]{2,3,1,0:T(8,128)(2,1)S(1)}, bf16[4,4,1024,5]{2,3,1,0:T(8,128)(2,1)S(1)}, u32[]{:S(2)}, u32[]{:S(2)}) %collective-permute-start) | collective-permute-done | bytes 163872 | tf_op jit(solution)/shard_map/ppermute | solution.py:37
  30.0 4.8 collective-permute-done.1
  34.7 5.5 pad_maximum_fusion
  40.3 3.5 copy-done
  47.7 18.5 %concatenate.17 = bf16[4,4,1034,266]{2,3,1,0:T(8,128)(2,1)} concatenate(bf16[4,4,5,266]{2,3,1,0:T(8,128)(2,1)S(1)} %copy.53, bf16[4,4,1024,266]{2,3,1,0:T(8,128)(2,1)} %copy-done, bf16[4,4,5,266]{2,3,1,0:T(8,128)(2,1)S(1)} %copy.54), dimensions={2} | concatenate | bytes 17602816 | tf_op jit(solution)/shard_map/concatenate | solution.py:39
  66.2 10.5 %fusion.5 = f32[4,4,1034,2,64]{2,4,1,0,3:T(8,128)S(1)} fusion(f32[266,2,64,1,1]{0,2,4,3,1:T(8,128)S(1)} %copy-done.5, bf16[4,4,1034,266]{2,3,1,0:T(8,128)(2,1)} %concatenate.17), kind=kOutput, calls=%fused_computation.17 | convolution fusion | flops 6759481344 | bytes 17408128 | tf_op jit(solution)/shard_map/cpxz,zsn->cpxsn/dot_general | solution.py:88
  76.7 8.7 %convolution_bitcast_fusion.1 = f32[2,4,4,256,64]{3,4,2,1,0:T(8,128)S(1)} fusion(f32[4,4,1034,2,64]{2,4,1,0,3:T(8,128)S(1)} %fusion.5, f32[2,1034,256,1,1]{2,1,4,3,0:T(8,128)S(1)} %copy-done.3), kind=kOutput, calls=%fused_computation.20 | convolution fusion | flops 6505365504 | bytes 12685312 | tf_op jit(solution)/shard_map/cpxsn,sxm->scpmn/dot_general | solution.py:89
  85.4 1.3 copy-done.1
  89.5 1.3 slice.46
  91.3 1.5 reshape.109
  94.4 2.3 reshape.96
  97.4 39.6 %all-gather.18.cloned.1.call-done = bf16[4,4,65536]{2,1,0:T(4,128)(2,1)} async-done(((bf16[1,4,65536]{2,1,0:T(4,128)(2,1)}), bf16[4,4,65536]{2,1,0:T(4,128)(2,1)}) %all-gather.18.cloned.1.call-update) | async-done | bytes 2097168 | tf_op jit(solution)/shard_map/all_gather | solution.py:108
  137.1 2.8 reshape.108
  139.9 43.4 %all-gather.20.cloned.1.call-done = bf16[4,4,65536]{2,1,0:T(4,128)(2,1)} async-done(((bf16[1,4,65536]{2,1,0:T(4,128)(2,1)}), bf16[4,4,65536]{2,1,0:T(4,128)(2,1)}) %all-gather.20.cloned.1.call-update) | async-done | bytes 2097168 | tf_op jit(solution)/shard_map/all_gather | solution.py:107
  183.3 2.8 reshape.110
  186.1 53.2 %while.30 = (s32[]{:T(128)}, f32[64,256]{1,0:T(8,128)S(1)}, f32[64,6]{0,1:T(8,128)S(1)}, bf16[4,65536]{1,0:T(4,128)(2,1)S(1)}, bf16[16,65536]{1,0:T(8,128)(2,1)}...) while((s32[]{:T(128)}, f32[64,256]{1,0:T(8,128)S(1)}, ...), condition=%wide.region_1.0_spmd.clone, body=%wide.region_0.0_spmd.clone.sunk | while | flops 140165888 | bytes 7703730 | solution.py:128
  240.0 6.9 %psum.141 = f32[64,6]{0,1:T(8,128)S(1)} all-reduce(f32[64,6]{0,1:T(8,128)S(1)} %get-tuple-element.237), channel_id=1, replica_groups=mesh['groups'=2,'cols'=4,'slab'=2,'rep'=2] {'slab','rep'}, use_global_device_ids=true, to_apply=%region_3.0 | all-reduce | flops 384 | bytes 3072 | tf_op jit(solution)/shard_map/psum | solution.py:134
  247.0 13.1 %all-gather.2 = f32[4,64,6]{1,2,0:T(8,128)S(1)} all-gather(f32[1,64,6]{1,2,0:T(8,128)S(1)} %fusion.29), channel_id=1, replica_groups=mesh['groups'=2,'cols'=4,'slab'=2,'rep'=2] {'cols'}, dimensions={0}, use_global_device_ids=true | all-gather | bytes 7680 | tf_op jit(solution)/shard_map/all_gather | solution.py:147
  260.1 3.8 collective-permute-start.6
  265.2 4.1 collective-permute-done.5
  271.9 11.6 %all-reduce = f32[256]{0:T(256)S(1)} all-reduce(f32[256]{0:T(256)S(1)} %dynamic-update-slice), channel_id=1, replica_groups=mesh['groups'=2,'cols'=4,'slab'=2,'rep'=2] {'cols'}, use_global_device_ids=true, to_apply=%add | all-reduce | flops 256 | bytes 2048
  284.8 13.1 %all-gather.3 = f32[4,64,6]{1,2,0:T(8,128)S(1)} all-gather(f32[1,64,6]{1,2,0:T(8,128)S(1)} %multiply_bitcast_fusion.10), channel_id=1, replica_groups=mesh['groups'=2,'cols'=4,'slab'=2,'rep'=2] {'cols'}, dimensions={0}, use_global_device_ids=true | all-gather | bytes 7680 | tf_op jit(solution)/shard_map/all_gather | solution.py:147
  299.2 8.4 %all-reduce.3 = (f32[6]{0:T(128)S(1)}, f32[6]{0:T(128)S(1)}) all-reduce(f32[6]{0:T(128)S(1)} %get-tuple-element.274, f32[6]{0:T(128)S(1)} %get-tuple-element.273), channel_id=1, replica_groups=mesh['groups'=2,'cols'=4,'slab'=2,'rep'=2] {'cols'}, use_global_device_ids=true, to_apply=%region_5.6 | all-reduce | flops 12 | bytes 96 | tf_op jit(solution)/shard_map/psum | solution.py:152
  307.8 10.4 %psum.144 = f32[6]{0:T(128)S(1)} all-reduce(f32[6]{0:T(128)S(1)} %get-tuple-element.327), channel_id=1, replica_groups=mesh['groups'=2,'cols'=4,'slab'=2,'rep'=2] {'cols'}, use_global_device_ids=true, to_apply=%region_9.10 | all-reduce | flops 6 | bytes 48 | tf_op jit(solution)/shard_map/psum | solution.py:152
  318.3 13.1 %all-gather.4 = f32[4,64,6]{1,2,0:T(8,128)S(1)} all-gather(f32[1,64,6]{1,2,0:T(8,128)S(1)} %get-tuple-element.325), channel_id=1, replica_groups=mesh['groups'=2,'cols'=4,'slab'=2,'rep'=2] {'cols'}, dimensions={0}, use_global_device_ids=true | all-gather | bytes 7680 | tf_op jit(solution)/shard_map/all_gather | solution.py:147
  332.7 8.4 %psum.145 = f32[6]{0:T(128)S(1)} all-reduce(f32[6]{0:T(128)S(1)} %get-tuple-element.341), channel_id=1, replica_groups=mesh['groups'=2,'cols'=4,'slab'=2,'rep'=2] {'cols'}, use_global_device_ids=true, to_apply=%region_11.12 | all-reduce | flops 6 | bytes 48 | tf_op jit(solution)/shard_map/psum | solution.py:166
  341.2 10.4 %psum.146 = f32[6]{0:T(128)S(1)} all-reduce(f32[6]{0:T(128)S(1)} %multiply_reduce_fusion.10), channel_id=1, replica_groups=mesh['groups'=2,'cols'=4,'slab'=2,'rep'=2] {'cols'}, use_global_device_ids=true, to_apply=%region_13.14 | all-reduce | flops 6 | bytes 48 | tf_op jit(solution)/shard_map/psum | solution.py:152
  351.7 13.1 %all-gather.5 = f32[4,64,6]{1,2,0:T(8,128)S(1)} all-gather(f32[1,64,6]{1,2,0:T(8,128)S(1)} %get-tuple-element.323), channel_id=1, replica_groups=mesh['groups'=2,'cols'=4,'slab'=2,'rep'=2] {'cols'}, dimensions={0}, use_global_device_ids=true | all-gather | bytes 7680 | tf_op jit(solution)/shard_map/all_gather | solution.py:147
  366.1 8.4 %psum.147 = f32[6]{0:T(128)S(1)} all-reduce(f32[6]{0:T(128)S(1)} %fusion.25), channel_id=1, replica_groups=mesh['groups'=2,'cols'=4,'slab'=2,'rep'=2] {'cols'}, use_global_device_ids=true, to_apply=%region_15.16 | all-reduce | flops 6 | bytes 48 | tf_op jit(solution)/shard_map/psum | solution.py:166
  374.6 13.1 %all-gather.6 = f32[4,64,6]{1,2,0:T(8,128)S(1)} all-gather(f32[1,64,6]{1,2,0:T(8,128)S(1)} %get-tuple-element.321), channel_id=1, replica_groups=mesh['groups'=2,'cols'=4,'slab'=2,'rep'=2] {'cols'}, dimensions={0}, use_global_device_ids=true | all-gather | bytes 7680 | tf_op jit(solution)/shard_map/all_gather | solution.py:147
  388.9 13.1 %all-gather.7 = f32[4,64,6]{1,2,0:T(8,128)S(1)} all-gather(f32[1,64,6]{1,2,0:T(8,128)S(1)} %multiply_bitcast_fusion.6), channel_id=1, replica_groups=mesh['groups'=2,'cols'=4,'slab'=2,'rep'=2] {'cols'}, dimensions={0}, use_global_device_ids=true | all-gather | bytes 7680 | tf_op jit(solution)/shard_map/all_gather | solution.py:147
  403.4 10.4 %all-reduce.2 = (f32[6]{0:T(128)S(1)}, f32[6]{0:T(128)S(1)}) all-reduce(f32[6]{0:T(128)S(1)} %get-tuple-element.272, f32[6]{0:T(128)S(1)} %get-tuple-element.271), channel_id=1, replica_groups=mesh['groups'=2,'cols'=4,'slab'=2,'rep'=2] {'cols'}, use_global_device_ids=true, to_apply=%region_17.18 | all-reduce | flops 12 | bytes 96 | tf_op jit(solution)/shard_map/psum | solution.py:152
  414.0 8.4 %psum.150 = f32[6]{0:T(128)S(1)} all-reduce(f32[6]{0:T(128)S(1)} %get-tuple-element.319), channel_id=1, replica_groups=mesh['groups'=2,'cols'=4,'slab'=2,'rep'=2] {'cols'}, use_global_device_ids=true, to_apply=%region_21.22 | all-reduce | flops 6 | bytes 48 | tf_op jit(solution)/shard_map/psum | solution.py:152
  422.4 13.1 %all-gather.8 = f32[4,64,6]{1,2,0:T(8,128)S(1)} all-gather(f32[1,64,6]{1,2,0:T(8,128)S(1)} %get-tuple-element.317), channel_id=1, replica_groups=mesh['groups'=2,'cols'=4,'slab'=2,'rep'=2] {'cols'}, dimensions={0}, use_global_device_ids=true | all-gather | bytes 7680 | tf_op jit(solution)/shard_map/all_gather | solution.py:147
  436.8 10.4 %psum.151 = f32[6]{0:T(128)S(1)} all-reduce(f32[6]{0:T(128)S(1)} %get-tuple-element.344), channel_id=1, replica_groups=mesh['groups'=2,'cols'=4,'slab'=2,'rep'=2] {'cols'}, use_global_device_ids=true, to_apply=%region_23.24 | all-reduce | flops 6 | bytes 48 | tf_op jit(solution)/shard_map/psum | solution.py:166
  447.4 8.4 %psum.152 = f32[6]{0:T(128)S(1)} all-reduce(f32[6]{0:T(128)S(1)} %multiply_reduce_fusion.5), channel_id=1, replica_groups=mesh['groups'=2,'cols'=4,'slab'=2,'rep'=2] {'cols'}, use_global_device_ids=true, to_apply=%region_25.26 | all-reduce | flops 6 | bytes 48 | tf_op jit(solution)/shard_map/psum | solution.py:152
  455.9 13.1 %all-gather.9 = f32[4,64,6]{1,2,0:T(8,128)S(1)} all-gather(f32[1,64,6]{1,2,0:T(8,128)S(1)} %get-tuple-element.315), channel_id=1, replica_groups=mesh['groups'=2,'cols'=4,'slab'=2,'rep'=2] {'cols'}, dimensions={0}, use_global_device_ids=true | all-gather | bytes 7680 | tf_op jit(solution)/shard_map/all_gather | solution.py:147
  470.3 10.4 %psum.153 = f32[6]{0:T(128)S(1)} all-reduce(f32[6]{0:T(128)S(1)} %fusion.26), channel_id=1, replica_groups=mesh['groups'=2,'cols'=4,'slab'=2,'rep'=2] {'cols'}, use_global_device_ids=true, to_apply=%region_27.28 | all-reduce | flops 6 | bytes 48 | tf_op jit(solution)/shard_map/psum | solution.py:166
  480.7 13.1 %all-gather.10 = f32[4,64,6]{1,2,0:T(8,128)S(1)} all-gather(f32[1,64,6]{1,2,0:T(8,128)S(1)} %get-tuple-element.313), channel_id=1, replica_groups=mesh['groups'=2,'cols'=4,'slab'=2,'rep'=2] {'cols'}, dimensions={0}, use_global_device_ids=true | all-gather | bytes 7680 | tf_op jit(solution)/shard_map/all_gather | solution.py:147
  494.3 13.1 %all-gather.11 = f32[4,64,6]{1,2,0:T(8,128)S(1)} all-gather(f32[1,64,6]{1,2,0:T(8,128)S(1)} %multiply_bitcast_fusion.2), channel_id=1, replica_groups=mesh['groups'=2,'cols'=4,'slab'=2,'rep'=2] {'cols'}, dimensions={0}, use_global_device_ids=true | all-gather | bytes 7680 | tf_op jit(solution)/shard_map/all_gather | solution.py:147
  507.8 8.4 %all-reduce.1 = (f32[6]{0:T(128)S(1)}, f32[6]{0:T(128)S(1)}) all-reduce(f32[6]{0:T(128)S(1)} %get-tuple-element.270, f32[6]{0:T(128)S(1)} %get-tuple-element.269), channel_id=1, replica_groups=mesh['groups'=2,'cols'=4,'slab'=2,'rep'=2] {'cols'}, use_global_device_ids=true, to_apply=%region_29.30 | all-reduce | flops 12 | bytes 96 | tf_op jit(solution)/shard_map/psum | solution.py:152
  516.4 10.4 %psum.156 = f32[6]{0:T(128)S(1)} all-reduce(f32[6]{0:T(128)S(1)} %get-tuple-element.311), channel_id=1, replica_groups=mesh['groups'=2,'cols'=4,'slab'=2,'rep'=2] {'cols'}, use_global_device_ids=true, to_apply=%region_33.34 | all-reduce | flops 6 | bytes 48 | tf_op jit(solution)/shard_map/psum | solution.py:152
  526.9 13.1 %all-gather.12 = f32[4,64,6]{1,2,0:T(8,128)S(1)} all-gather(f32[1,64,6]{1,2,0:T(8,128)S(1)} %get-tuple-element.309), channel_id=1, replica_groups=mesh['groups'=2,'cols'=4,'slab'=2,'rep'=2] {'cols'}, dimensions={0}, use_global_device_ids=true | all-gather | bytes 7680 | tf_op jit(solution)/shard_map/all_gather | solution.py:147
  540.4 8.4 %psum.157 = f32[6]{0:T(128)S(1)} all-reduce(f32[6]{0:T(128)S(1)} %get-tuple-element.347), channel_id=1, replica_groups=mesh['groups'=2,'cols'=4,'slab'=2,'rep'=2] {'cols'}, use_global_device_ids=true, to_apply=%region_35.36 | all-reduce | flops 6 | bytes 48 | tf_op jit(solution)/shard_map/psum | solution.py:166
  549.0 10.4 %psum.158 = f32[6]{0:T(128)S(1)} all-reduce(f32[6]{0:T(128)S(1)} %multiply_reduce_fusion), channel_id=1, replica_groups=mesh['groups'=2,'cols'=4,'slab'=2,'rep'=2] {'cols'}, use_global_device_ids=true, to_apply=%region_37.38 | all-reduce | flops 6 | bytes 48 | tf_op jit(solution)/shard_map/psum | solution.py:152
  559.5 13.1 %all-gather.13 = f32[4,64,6]{1,2,0:T(8,128)S(1)} all-gather(f32[1,64,6]{1,2,0:T(8,128)S(1)} %get-tuple-element.307), channel_id=1, replica_groups=mesh['groups'=2,'cols'=4,'slab'=2,'rep'=2] {'cols'}, dimensions={0}, use_global_device_ids=true | all-gather | bytes 7680 | tf_op jit(solution)/shard_map/all_gather | solution.py:147
  573.0 8.4 %psum.159 = f32[6]{0:T(128)S(1)} all-reduce(f32[6]{0:T(128)S(1)} %fusion.27), channel_id=1, replica_groups=mesh['groups'=2,'cols'=4,'slab'=2,'rep'=2] {'cols'}, use_global_device_ids=true, to_apply=%region_39.40 | all-reduce | flops 6 | bytes 48 | tf_op jit(solution)/shard_map/psum | solution.py:166
  581.5 13.4 %all-gather.14 = f32[4,64,6]{1,2,0:T(8,128)S(1)} all-gather(f32[1,64,6]{1,2,0:T(8,128)S(1)} %bitcast.243), channel_id=1, replica_groups=mesh['groups'=2,'cols'=4,'slab'=2,'rep'=2] {'cols'}, dimensions={0}, use_global_device_ids=true | all-gather | bytes 7680 | tf_op jit(solution)/shard_map/all_gather | solution.py:174
  595.1 41.2 %while.29 = (s32[]{:T(128)}, bf16[6,65536]{1,0:T(8,128)(2,1)S(1)}, bf16[6,65536]{1,0:T(8,128)(2,1)}, bf16[16,65536]{1,0:T(8,128)(2,1)}, bf16[16,65536]{1,0:T(8,1...) while((s32[]{:T(128)}, bf16[6,65536]{1,0:T(8,128)(2,1)S(1)}, ...), condition=%wide.region_41.42_spmd, body=%wide.region_40.41_spmd.sunk | while | flops 14884870 | bytes 5623963 | solution.py:188
  596.4 1.2 fusion.73
  601.6 1.2 fusion.73
  604.2 1.2 fusion.73
  606.7 1.2 fusion.73
  611.9 1.2 fusion.73
  614.4 1.2 fusion.73
  617.0 1.2 fusion.73
  622.2 1.2 fusion.73
  624.7 1.2 fusion.73
  632.4 1.2 fusion.73
  635.0 1.2 fusion.73
  636.3 1.6 reshape.97
  637.9 1.4 copy.72
  (271 shorter events, 109.2 us)
Async XLA Ops:
  7.2 129.9 %all-gather.18.cloned.1.call-start = ((), (), s32[]{:S(2)}) async-start(), calls=%async_computation.1 | async-start | bytes 2621440 | tf_op jit(solution)/shard_map/all_gather | solution.py:108
  19.8 10.1 %collective-permute-start = (bf16[4,4,1024,5]{2,3,1,0:T(8,128)(2,1)S(1)}, bf16[4,4,1024,5]{2,3,1,0:T(8,128)(2,1)S(1)}, u32[]{:S(2)}, u32[]{:S(2)}) collective-permute-start(bf16[4,4,1024,5]{2,3,1,0:T(8,128)(2,1)S(1)} %get-tuple-element.335), channel_id=1, source_target_pairs={{0,2},{2,0},{1,3},{3,1},{4,6},{6,4},{5,7},{7,5},{8,10},{10,8},{9,1... | collective-permute-start | bytes 491528 | tf_op jit(solution)/shard_map/ppermute | solution.py:37
  22.8 11.9 %collective-permute-start.1 = (bf16[4,4,1024,5]{2,3,1,0:T(8,128)(2,1)S(1)}, bf16[4,4,1024,5]{2,3,1,0:T(8,128)(2,1)S(1)}, u32[]{:S(2)}, u32[]{:S(2)}) collective-permute-start(bf16[4,4,1024,5]{2,3,1,0:T(8,128)(2,1)S(1)} %get-tuple-element.336), channel_id=1, source_target_pairs={{2,0},{0,2},{3,1},{1,3},{6,4},{4,6},{7,5},{5,7},{10,8},{8,10},{11,... | collective-permute-start | bytes 491528 | tf_op jit(solution)/shard_map/ppermute | solution.py:38
  40.3 3.5 copy-start
  44.4 1.8 copy-start.8
  45.0 1.5 collective-permute-start.2
  45.6 1.5 collective-permute-start.3
  47.7 18.5 %copy-start.5 = (f32[266,2,64,1,1]{0,2,4,3,1:T(8,128)S(1)}, f32[266,2,64,1,1]{0,2,4,3,1:T(8,128)}, u32[]{:S(2)}) copy-start(f32[266,2,64,1,1]{0,2,4,3,1:T(8,128)} %constant.156) | copy-start | bytes 408580
  66.2 10.5 %copy-start.3 = (f32[2,1034,256,1,1]{2,1,4,3,0:T(8,128)S(1)}, f32[2,1034,256,1,1]{2,1,4,3,0:T(8,128)}, u32[]{:S(2)}) copy-start(f32[2,1034,256,1,1]{2,1,4,3,0:T(8,128)} %constant.157) | copy-start | bytes 6352900
  85.4 1.4 copy-start.1
  89.4 3.7 copy-start.4
  89.4 93.9 %all-gather.20.cloned.1.call-start = ((), (), s32[]{:S(2)}) async-start(), calls=%async_computation.2 | async-start | bytes 2621440 | tf_op jit(solution)/shard_map/all_gather | solution.py:107
  92.8 177.1 %all-reduce.6.cloned.1.call-start = ((), (), s32[]{:S(2)}) async-start(), calls=%async_computation | async-start | bytes 131072 | tf_op jit(solution)/shard_map/psum | solution.py:134
  93.5 3.2 copy-start.6
  186.1 77.9 %copy-start.9 = (u32[32]{0:T(128)S(1)}, u32[32]{0:T(128)}, u32[]{:S(2)}) copy-start(u32[32]{0:T(128)} %constant.152) | copy-start | bytes 388
  239.3 0.6 copy-start.2
  246.9 17.0 %collective-permute-start.4 = (f32[64,6]{0,1:T(8,128)S(1)}, f32[64,6]{0,1:T(8,128)S(1)}, u32[]{:S(2)}, u32[]{:S(2)}) collective-permute-start(f32[64,6]{0,1:T(8,128)S(1)} %psum.141), channel_id=1, source_target_pairs={{0,4},{4,8},{8,12},{12,0},{1,5},{5,9},{9,13},{13,1},{2,6},{6,10},{... | collective-permute-start | bytes 4616 | tf_op jit(solution)/shard_map/ppermute | solution.py:23
  260.1 5.2 collective-permute-start.6
  263.9 5.4 collective-permute-start.5
  270.0 224.0 %copy-start.7 = (f32[64,256]{1,0:T(8,128)S(1)}, f32[64,256]{1,0:T(8,128)}, u32[]{:S(2)}) copy-start(f32[64,256]{1,0:T(8,128)} %all-reduce.6.cloned.1.call-done) | copy-start | bytes 196612
Sparse Core Ops, SparseCore 0:
  89.5 47.4 all-gather.17
  138.6 44.6 all-gather.19
  240.1 29.8 all-reduce.5
